TPU v7x, 32 devices: a whole 2x2x4 slice. The times are simulated.
32 devices in a mesh: tm: 4 (over y, x), chan: 8 (over z, core).
Axes of the slice: x: 2, y: 2, z: 4, core: 2. Of those that a mesh axis runs over, the one named last changes fastest.
Arguments:
- strain: bfloat16 [256, 16384], P('chan', 'tm'), may hold values from -6 to 6
- fir_taps: bfloat16 [256, 256], P('chan'), may hold values from -0.375 to 0.375
Outputs:
- stacked: float32 [2, 256, 256, 256], P(None, 'tm', 'chan')
All inputs are finite; a program needn't handle non-finite values.
Results may differ from a plain program's by a relative error of at most 0.0062.
Values may be sent and summed in bfloat16 or wider, within the bound.
No kernel may reach another device: no remote copies, remote signals or barrier semaphores. Data moves between devices by JAX's collectives and lax.ppermute only.
A program may use at most 128 MiB of HBM per device.

v0:
```python
import math
import jax
import jax.numpy as jnp
from jax import lax
from jax.sharding import PartitionSpec as P

SEG = 512


def shifted(value, axis, by):
    size = lax.axis_size(axis)
    pairs = [(i, i + by) for i in range(size) if 0 <= i + by < size]
    return lax.ppermute(value, axis, pairs)


def make_table():
    sample_idx = jnp.arange(SEG, dtype=jnp.int32)
    bin_idx = jnp.arange(SEG // 2, dtype=jnp.int32)
    phases = sample_idx[:, None] * bin_idx[None, :] % SEG
    angles = phases.astype(jnp.float32) * (2.0 * math.pi / SEG)
    window = 0.5 - 0.5 * jnp.cos(sample_idx.astype(jnp.float32) * (2.0 * math.pi / SEG))
    cosine = window[:, None] * jnp.cos(angles)
    sine_part = -window[:, None] * jnp.sin(angles)
    return jnp.stack([cosine, sine_part], axis=1).astype(jnp.bfloat16)


def toeplitz(fir_taps):
    tap_count = fir_taps.shape[1]
    row_idx = jnp.arange(2 * tap_count, dtype=jnp.int32)[:, None]
    col_idx = jnp.arange(tap_count, dtype=jnp.int32)[None, :]
    lag_idx = col_idx + tap_count - row_idx
    valid = (lag_idx >= 0) & (lag_idx < tap_count)
    picked = jnp.take(fir_taps, jnp.clip(lag_idx, 0, tap_count - 1), axis=1)
    return jnp.where(valid[None, :, :], picked, jnp.zeros_like(picked))


def cross_block(own_bins, other_bins):
    swapped = jnp.stack([-other_bins[:, 1], other_bins[:, 0]], axis=1)
    real_part = jnp.einsum(
        "kpsi,kpsj->kij", own_bins, other_bins, preferred_element_type=jnp.float32
    )
    imag_part = jnp.einsum("kpsi,kpsj->kij", own_bins, swapped, preferred_element_type=jnp.float32)
    return jnp.stack([real_part, imag_part], axis=0)


def shards(strain, fir_taps):
    tap_count = fir_taps.shape[1]
    channels = strain.shape[0]
    previous = shifted(strain[:, -tap_count:], "tm", 1)
    extended = jnp.concatenate([previous, strain], axis=1)[:, 1:]
    filtered = lax.conv_general_dilated(
        extended[None],
        jnp.flip(fir_taps, axis=1)[:, None, :],
        window_strides=(1,),
        padding="VALID",
        dimension_numbers=("NCH", "OIH", "NCH"),
        feature_group_count=channels,
        preferred_element_type=jnp.float32,
    )[0]
    whitened = filtered.reshape(channels, -1).astype(jnp.bfloat16)
    segments = whitened.reshape(channels, whitened.shape[1] // SEG, SEG)
    spectra = jnp.einsum(
        "csn,npk->kpsc", segments, make_table(), preferred_element_type=jnp.float32
    ).astype(jnp.bfloat16)
    gathered = lax.all_gather(spectra, "chan", axis=3, tiled=True)
    all_bins = lax.all_to_all(gathered, "tm", split_axis=0, concat_axis=2, tiled=True)
    factor = 1.0 / (all_bins.shape[2] * SEG)
    first_col = lax.axis_index("chan") * channels
    own_bins = lax.dynamic_slice_in_dim(all_bins, first_col, channels, 3)
    result = cross_block(own_bins, all_bins) * factor
    return result


def solution(mesh):
    placed = (P("chan", "tm"), P("chan", None))
    return jax.shard_map(
        shards, mesh=mesh, in_specs=placed, out_specs=P(None, "tm", "chan", None), check_vma=False
    )
```

profile of v0, /device:TPU:0, one launch (start us, length us, event | category | flops | bytes accessed | tf_op | source)
XLA Modules:
  0.0 157.0 jit_solution(7761917013179768277)
XLA Ops:
  6.5 0.0 all-gather.2.cloned.1.call-start
  6.5 0.7 slice.12
  7.3 4.8 %collective-permute-start = (bf16[32,256]{1,0:T(8,128)(2,1)S(1)}, bf16[32,256]{1,0:T(8,128)(2,1)S(1)}, u32[]{:S(2)}, u32[]{:S(2)}) collective-permute-start(bf16[32,256]{1,0:T(8,128)(2,1)S(1)} %slice.12), channel_id=1, source_target_pairs={{0,8},{8,16},{16,24},{1,9},{9,17},{17,25},{2,10},{10,18},{18,26},{... | collective-permute-start | bytes 49160 | tf_op jit(solution)/shard_map/ppermute | solution.py:13
  12.2 2.3 %multiply_convert_fusion = (bf16[512,1,256]{2,0,1:T(8,128)(2,1)S(1)}, bf16[512,1,256]{2,0,1:T(8,128)(2,1)S(1)}) fusion(f32[512]{0:T(512)S(1)} %fusion.30, f32[512]{0:T(512)S(1)} %multiply_subtract_fusion), kind=kLoop, calls=%fused_computation.32 | loop fusion | flops 2359296 | bytes 528384 | tf_op jit(solution)/shard_map/convert.1
  14.5 0.9 rev.4
  15.4 0.1 copy.37
  15.5 0.0 collective-permute-done
  15.5 1.1 fusion.27
  16.6 0.6 reshape.125
  17.2 0.9 copy.36
  18.1 0.1 slice.18
  18.2 0.4 fusion.43
  18.6 0.0 copy-start
  18.6 61.0 %fusion.7 = bf16[8,544,32]{2,0,1:T(8,128)(2,1)S(1)} fusion(bf16[32,1,256]{0,1,2:T(2,128)(2,1)S(1)} %copy.37, bf16[32,8,799]{0,1,2:T(8,128)(2,1)S(1)} %fusion.43), kind=kOutput, calls=%fused_computation.10 | convolution fusion | flops 71303168 | bytes 704000 | tf_op jit(solution)/shard_map/conv_general_dilated | solution.py:51
  79.6 0.8 copy.38
  80.4 0.0 copy-done
  80.4 0.1 select_convert_fusion
  80.5 0.1 copy.39
  80.6 0.3 reshape.129
  80.9 0.1 copy.50
  81.0 1.0 fusion.15
  82.0 0.0 all-gather.2.cloned.1.call-update
  82.0 29.6 %all-gather.2.cloned.1.call-done = bf16[256,2,8,256]{0,3,2,1:T(8,128)(2,1)} async-done(((bf16[256,2,8,32]{0,3,2,1:T(8,128)(2,1)}), bf16[256,2,8,256]{0,3,2,1:T(8,128)(2,1)}) %all-gather.2.cloned.1.call-update) | async-done | bytes 2097168 | tf_op jit(solution)/shard_map/all_gather | solution.py:65
  111.6 4.5 %copy.41 = bf16[256,2,8,256]{3,2,1,0:T(8,128)(2,1)} copy(bf16[256,2,8,256]{0,3,2,1:T(8,128)(2,1)} %all-gather.2.cloned.1.call-done) | data formatting | bytes 4194304 | tf_op jit(solution)/shard_map/all_gather | solution.py:65
  116.1 3.6 %all-to-all-start = ((bf16[256,2,8,256]{3,2,1,0:T(8,128)(2,1)}), bf16[256,2,8,256]{3,2,1,0:T(8,128)(2,1)S(1)}, u32[]{:S(2)}, u32[]{:S(2)}) async-start(bf16[256,2,8,256]{3,2,1,0:T(8,128)(2,1)} %copy.41), calls=%async_computation | async-start | bytes 4194304 | tf_op jit(solution)/shard_map/all_to_all | solution.py:66
  119.7 25.5 %all-to-all-done = bf16[256,2,8,256]{3,2,1,0:T(8,128)(2,1)S(1)} async-done(((bf16[256,2,8,256]{3,2,1,0:T(8,128)(2,1)}), bf16[256,2,8,256]{3,2,1,0:T(8,128)(2,1)S(1)}, u32[]{:S(2)}, u32[]{:S(2)}) %all-to-all-start) | async-done | bytes 2097184 | tf_op jit(solution)/shard_map/all_to_all | solution.py:66
  145.2 0.3 copy.56
  145.5 0.1 slice_negate_fusion
  145.7 1.0 convolution_bitcast_fusion
  146.7 1.0 fusion.12
  147.7 2.5 %maximum_multiply_fusion = f32[2,64,32,256]{3,2,1,0:T(8,128)} fusion(f32[1,64,32,256]{3,2,1,0:T(8,128)S(1)} %fusion.12, f32[1,64,32,256]{3,2,1,0:T(8,128)S(1)} %convolution_bitcast_fusion), kind=kLoop, calls=%fused_computation | loop fusion | flops 2097152 | bytes 8388608 | tf_op jit(solution)/shard_map/mul | solution.py:70
  (4 shorter events, 0.1 us)
Async XLA Ops:
  6.5 105.1 %all-gather.2.cloned.1.call-start = ((), (), s32[]{:S(2)}) async-start(), calls=%async_computation.1 | async-start | bytes 2359296 | tf_op jit(solution)/shard_map/all_gather | solution.py:65
  7.3 8.3 %collective-permute-start = (bf16[32,256]{1,0:T(8,128)(2,1)S(1)}, bf16[32,256]{1,0:T(8,128)(2,1)S(1)}, u32[]{:S(2)}, u32[]{:S(2)}) collective-permute-start(bf16[32,256]{1,0:T(8,128)(2,1)S(1)} %slice.12), channel_id=1, source_target_pairs={{0,8},{8,16},{16,24},{1,9},{9,17},{17,25},{2,10},{10,18},{18,26},{... | collective-permute-start | bytes 49160 | tf_op jit(solution)/shard_map/ppermute | solution.py:13
  18.6 61.8 %copy-start = (pred[8,544]{1,0:T(8,128)(4,1)S(1)}, pred[8,544]{1,0:T(8,128)(4,1)}, u32[]{:S(2)}) copy-start(pred[8,544]{1,0:T(8,128)(4,1)} %constant.37) | copy-start | bytes 13060
  116.1 29.1 %all-to-all-start = ((bf16[256,2,8,256]{3,2,1,0:T(8,128)(2,1)}), bf16[256,2,8,256]{3,2,1,0:T(8,128)(2,1)S(1)}, u32[]{:S(2)}, u32[]{:S(2)}) async-start(bf16[256,2,8,256]{3,2,1,0:T(8,128)(2,1)} %copy.41), calls=%async_computation | async-start | bytes 4194304 | tf_op jit(solution)/shard_map/all_to_all | solution.py:66
Sparse Core Ops, SparseCore 0:
  82.1 29.4 all-gather.1
where the time goes:
time: 157 us
  matrix products  64.1 us (41%)
  waiting for transfers between devices  55.1 us (35%)
  between operations  13.6 us (9%)
  local copies, waits for them, and re-layouts  9.31 us (6%)
  starting transfers between devices  8.48 us (5%)
  other arithmetic  6.53 us (4%)
    conv_general_dilated x1, matrix products, shards(): lax.conv_general_dilated(extended[None], jnp.flip(fir_taps, axis=1)[:, No...  61 us
    all_gather x1, waiting for transfers between devices, shards(): gathered = lax.all_gather(spectra, 'chan', axis=3, tiled=True)  29.6 us
    all_to_all x1, waiting for transfers between devices, shards(): lax.all_to_all(gathered, 'tm', split_axis=0, concat_axis=2, tiled=True)  25.5 us
    ppermute x1, starting transfers between devices, shifted(): return lax.ppermute(value, axis, pairs)  4.83 us
    all_gather x1, local copies, waits for them, and re-layouts, shards(): gathered = lax.all_gather(spectra, 'chan', axis=3, tiled=True)  4.49 us
    all_to_all x1, starting transfers between devices, shards(): lax.all_to_all(gathered, 'tm', split_axis=0, concat_axis=2, tiled=True)  3.65 us
  transfers between devices with their start and end apart: 3, of which 2 were waited for; matrix products, arithmetic and copies ran while one was open for 2% of the time, Pallas kernels for 0%

commit v1 on v0

--- a/solution.py
+++ b/solution.py
@@ -63,7 +63,10 @@
         "csn,npk->kpsc", segments, make_table(), preferred_element_type=jnp.float32
     ).astype(jnp.bfloat16)
     gathered = lax.all_gather(spectra, "chan", axis=3, tiled=True)
-    all_bins = lax.all_to_all(gathered, "tm", split_axis=0, concat_axis=2, tiled=True)
+    all_bins = jnp.concatenate(
+        lax.all_to_all(jnp.stack(jnp.split(gathered, lax.axis_size("tm"), axis=0)), "tm", 0, 0),
+        axis=2,
+    )
     factor = 1.0 / (all_bins.shape[2] * SEG)
     first_col = lax.axis_index("chan") * channels
     own_bins = lax.dynamic_slice_in_dim(all_bins, first_col, channels, 3)

time: 157 us -> 164 us (1.045)
  local copies, waits for them, and re-layouts: 9.31 us -> 13.5 us
  other arithmetic: 6.53 us -> 9.11 us
    another operation x0 -> x2, local copies, waits for them, and re-layouts: none -> 8.66 us  [shards(): jnp.stack(jnp.split(gathered, lax.axis_size('tm'), axis=0))]
    all_gather x1 -> x0, local copies, waits for them, and re-layouts: 4.49 us -> none  [shards(): gathered = lax.all_gather(spectra, 'chan', axis=3, tiled=True)]
    another operation x1 -> x2, other arithmetic: 2.31 us -> 4.9 us  [the longest x1 2.59 us: shards(): jnp.stack(jnp.split(gathered, lax.axis_size('tm'), axis=0))]
where the time goes in v1:
time: 164 us
  matrix products  64.1 us (39%)
  waiting for transfers between devices  55.1 us (34%)
  between operations  13.6 us (8%)
  local copies, waits for them, and re-layouts  13.5 us (8%)
  other arithmetic  9.11 us (6%)
  starting transfers between devices  8.48 us (5%)
    conv_general_dilated x1, matrix products, shards(): lax.conv_general_dilated(extended[None], jnp.flip(fir_taps, axis=1)[:, No...  61 us
    all_gather x1, waiting for transfers between devices, shards(): gathered = lax.all_gather(spectra, 'chan', axis=3, tiled=True)  29.6 us
    all_to_all x1, waiting for transfers between devices, shards(): lax.all_to_all(jnp.stack(jnp.split(gathered, lax.axis_size('tm'), axis=0)...  25.5 us
    another operation x2, local copies, waits for them, and re-layouts, shards(): jnp.stack(jnp.split(gathered, lax.axis_size('tm'), axis=0))  8.66 us
    ppermute x1, starting transfers between devices, shifted(): return lax.ppermute(value, axis, pairs)  4.83 us
    all_to_all x1, starting transfers between devices, shards(): lax.all_to_all(jnp.stack(jnp.split(gathered, lax.axis_size('tm'), axis=0)...  3.65 us
  transfers between devices with their start and end apart: 3, of which 2 were waited for; matrix products, arithmetic and copies ran while one was open for 2% of the time, Pallas kernels for 0%

profile of v1, /device:TPU:0, one launch (start us, length us, event | category | flops | bytes accessed | tf_op | source)
XLA Modules:
  0.0 163.8 jit_solution(16261302013762512850)
XLA Ops:
  6.5 0.0 all-gather.2.cloned.1.call-start
  6.5 0.7 slice.12
  7.3 4.8 %collective-permute-start = (bf16[32,256]{1,0:T(8,128)(2,1)S(1)}, bf16[32,256]{1,0:T(8,128)(2,1)S(1)}, u32[]{:S(2)}, u32[]{:S(2)}) collective-permute-start(bf16[32,256]{1,0:T(8,128)(2,1)S(1)} %slice.12), channel_id=1, source_target_pairs={{0,8},{8,16},{16,24},{1,9},{9,17},{17,25},{2,10},{10,18},{18,26},{... | collective-permute-start | bytes 49160 | tf_op jit(solution)/shard_map/ppermute | solution.py:13
  12.2 2.3 %multiply_convert_fusion = (bf16[512,1,256]{2,0,1:T(8,128)(2,1)S(1)}, bf16[512,1,256]{2,0,1:T(8,128)(2,1)S(1)}) fusion(f32[512]{0:T(512)S(1)} %fusion.30, f32[512]{0:T(512)S(1)} %multiply_subtract_fusion), kind=kLoop, calls=%fused_computation.37 | loop fusion | flops 2359296 | bytes 528384 | tf_op jit(solution)/shard_map/convert.1
  14.5 0.9 rev.4
  15.4 0.1 copy.32
  15.5 0.0 collective-permute-done
  15.5 1.1 fusion.27
  16.6 0.6 reshape.133
  17.2 0.9 copy.31
  18.1 0.1 slice.18
  18.2 0.4 fusion.43
  18.6 0.0 copy-start
  18.6 61.0 %fusion.7 = bf16[8,544,32]{2,0,1:T(8,128)(2,1)S(1)} fusion(bf16[32,1,256]{0,1,2:T(2,128)(2,1)S(1)} %copy.32, bf16[32,8,799]{0,1,2:T(8,128)(2,1)S(1)} %fusion.43), kind=kOutput, calls=%fused_computation.11 | convolution fusion | flops 71303168 | bytes 704000 | tf_op jit(solution)/shard_map/conv_general_dilated | solution.py:51
  79.6 0.8 copy.33
  80.4 0.1 select_convert_fusion
  80.5 0.1 copy.34
  80.6 0.3 reshape.137
  80.9 0.1 copy.43
  81.0 1.0 fusion.15
  82.0 0.0 all-gather.2.cloned.1.call-update
  82.0 29.6 %all-gather.2.cloned.1.call-done = bf16[256,2,8,256]{0,3,2,1:T(8,128)(2,1)} async-done(((bf16[256,2,8,32]{0,3,2,1:T(8,128)(2,1)}), bf16[256,2,8,256]{0,3,2,1:T(8,128)(2,1)}) %all-gather.2.cloned.1.call-update) | async-done | bytes 2097168 | tf_op jit(solution)/shard_map/all_gather | solution.py:65
  111.6 3.0 %slice_bitcast_fusion.3 = (bf16[1,64,2,8,256]{1,4,3,2,0:T(8,128)(2,1)S(1)}, bf16[1,64,2,8,256]{1,4,3,2,0:T(8,128)(2,1)S(1)}, bf16[1,64,2,8,256]{1,4,3,2,0:T(8,128)(2,1)S(1)}, bf16[1,64,2,8,256]{1,4,3,2,0:T(8,128)(2,1)S(1)}) fusion(bf16[256,2,8,256]{0,3,2,1:T(8,128)(2,1)} %all-gather.2.cloned.1.call-done), kind=kLoop, calls=%fused_computation.23 | loop fusion | bytes 4194304 | tf_op jit(solution)/shard_map/stack | solution.py:67
  114.6 2.6 %pad_maximum_fusion = bf16[4,64,2,8,256]{1,4,3,2,0:T(8,128)(2,1)} fusion(bf16[1,64,2,8,256]{1,4,3,2,0:T(8,128)(2,1)S(1)} %get-tuple-element.8, bf16[1,64,2,8,256]{1,4,3,2,0:T(8,128)(2,1)S(1)} %get-tuple-element.9, bf16[1,64,2,8,256]{1,4,3,2,0:T(8,128)(2,1)S(1)} %get-tuple-element.10, bf16[1,64,2,8,256]{1,4,3,2,0:T(8,128)(2,1)S(1)} %get-tuple-element.7), kind=kLoop, calls=%fused_computation | loop fusion | flops 3145728 | bytes 4194304 | tf_op jit(solution)/shard_map/stack | solution.py:67
  117.2 5.6 %copy.36 = bf16[4,64,2,8,256]{4,3,2,1,0:T(8,128)(2,1)} copy(bf16[4,64,2,8,256]{1,4,3,2,0:T(8,128)(2,1)} %pad_maximum_fusion) | data formatting | bytes 4194304 | tf_op jit(solution)/shard_map/stack | solution.py:67
  122.9 3.6 %all-to-all-start = ((bf16[4,64,2,8,256]{4,3,2,1,0:T(8,128)(2,1)}), bf16[4,64,2,8,256]{4,3,2,1,0:T(8,128)(2,1)S(1)}, u32[]{:S(2)}, u32[]{:S(2)}) async-start(bf16[4,64,2,8,256]{4,3,2,1,0:T(8,128)(2,1)} %copy.36), calls=%async_computation | async-start | bytes 4194304 | tf_op jit(solution)/shard_map/all_to_all | solution.py:67
  126.5 25.5 %all-to-all-done = bf16[4,64,2,8,256]{4,3,2,1,0:T(8,128)(2,1)S(1)} async-done(((bf16[4,64,2,8,256]{4,3,2,1,0:T(8,128)(2,1)}), bf16[4,64,2,8,256]{4,3,2,1,0:T(8,128)(2,1)S(1)}, u32[]{:S(2)}, u32[]{:S(2)}) %all-to-all-start) | async-done | bytes 2097184 | tf_op jit(solution)/shard_map/all_to_all | solution.py:67
  152.0 0.3 copy.49
  152.3 0.1 slice_negate_fusion
  152.4 1.0 convolution_bitcast_fusion
  153.4 1.0 fusion.12
  154.5 2.5 %maximum_multiply_fusion = f32[2,64,32,256]{3,2,1,0:T(8,128)} fusion(f32[1,64,32,256]{3,2,1,0:T(8,128)S(1)} %fusion.12, f32[1,64,32,256]{3,2,1,0:T(8,128)S(1)} %convolution_bitcast_fusion), kind=kLoop, calls=%fused_computation.1 | loop fusion | flops 2097152 | bytes 8388608 | tf_op jit(solution)/shard_map/mul | solution.py:73
  (5 shorter events, 0.1 us)
Async XLA Ops:
  6.5 105.1 %all-gather.2.cloned.1.call-start = ((), (), s32[]{:S(2)}) async-start(), calls=%async_computation.1 | async-start | bytes 2359296 | tf_op jit(solution)/shard_map/all_gather | solution.py:65
  7.3 8.3 %collective-permute-start = (bf16[32,256]{1,0:T(8,128)(2,1)S(1)}, bf16[32,256]{1,0:T(8,128)(2,1)S(1)}, u32[]{:S(2)}, u32[]{:S(2)}) collective-permute-start(bf16[32,256]{1,0:T(8,128)(2,1)S(1)} %slice.12), channel_id=1, source_target_pairs={{0,8},{8,16},{16,24},{1,9},{9,17},{17,25},{2,10},{10,18},{18,26},{... | collective-permute-start | bytes 49160 | tf_op jit(solution)/shard_map/ppermute | solution.py:13
  18.6 61.8 %copy-start = (pred[8,544]{1,0:T(8,128)(4,1)S(1)}, pred[8,544]{1,0:T(8,128)(4,1)}, u32[]{:S(2)}) copy-start(pred[8,544]{1,0:T(8,128)(4,1)} %constant.37) | copy-start | bytes 13060
  122.9 29.1 %all-to-all-start = ((bf16[4,64,2,8,256]{4,3,2,1,0:T(8,128)(2,1)}), bf16[4,64,2,8,256]{4,3,2,1,0:T(8,128)(2,1)S(1)}, u32[]{:S(2)}, u32[]{:S(2)}) async-start(bf16[4,64,2,8,256]{4,3,2,1,0:T(8,128)(2,1)} %copy.36), calls=%async_computation | async-start | bytes 4194304 | tf_op jit(solution)/shard_map/all_to_all | solution.py:67
Sparse Core Ops, SparseCore 0:
  82.1 29.4 all-gather.1
